TPU v7x, 512 devices: a whole 4x4x16 slice. The times are simulated.
512 devices in a mesh: gx: 32 (over z_hi, x, core), gy: 4 (over y), gz: 4 (over z_lo).
Axes of the slice: x: 4, y: 4, z: 16 (z_hi: 4, z_lo: 4; z = z_hi * 4 + z_lo), core: 2. Of those that a mesh axis runs over, the one named last changes fastest.
Arguments:
- level_set: float32 [1024, 128, 512], P('gx', 'gy', 'gz'), may hold values from -6 to 6
- velocity: bfloat16 [3, 1024, 128, 512], P(None, 'gx', 'gy', 'gz'), may hold values from -1 to 1
- active_brick: int32 [32, 4, 4], P('gx', 'gy', 'gz'), may hold values 0 or 1
- depth_order: int32 [4], replicated, may hold values from 0 to 3, as said below
Outputs:
- level_out: float32 [1024, 128, 512], P('gx', 'gy', 'gz')
- image: float32 [4, 2048, 256], P(None, ('gx', 'gz'), 'gy')
Inputs may be any that keep to these rules, and one draw needn't show every extreme that they name: `depth_order`: either 0, 1, .. in slab order or the reverse.
All inputs are finite; a program needn't handle non-finite values. No bound on the sum of `active_brick` on one device may be relied on, other than what follows from the above.
Results may differ from a plain program's by a relative error of at most 0.0003.
Values may be sent and summed in bfloat16 or wider, within the bound.
No kernel may reach another device: no remote copies, remote signals or barrier semaphores. Data moves between devices by JAX's collectives and lax.ppermute only.
A program may use at most 64 MiB of HBM per device.

v0:
```python
import jax
import jax.numpy as jnp
from jax import lax
from jax.sharding import PartitionSpec as P

CZ = 128
time_step = 0.4
weno_floor = 1e-06
SPAN = 3


def exchange(fields, axis, widths, dim):
    size = lax.axis_size(axis)
    up = [(i, (i + 1) % size) for i in range(size)]
    down = [(j, i) for i, j in up]
    out = []
    for field, w in zip(fields, widths):
        d = dim + field.ndim - 3
        last = lax.slice_in_dim(field, field.shape[d] - w, field.shape[d], axis=d)
        first = lax.slice_in_dim(field, 0, w, axis=d)
        before = lax.ppermute(last, axis, up)
        after = lax.ppermute(first, axis, down)
        out.append(jnp.concatenate([before, field, after], axis=d))
    return out


def exchange_packed(fields, axis, widths):
    size = lax.axis_size(axis)
    up = [(i, (i + 1) % size) for i in range(size)]
    down = [(j, i) for i, j in up]
    dims = [field.ndim - 3 for field in fields]
    lasts = [
        lax.slice_in_dim(field, field.shape[d] - w, field.shape[d], axis=d)
        for field, w, d in zip(fields, widths, dims)
    ]
    firsts = [lax.slice_in_dim(field, 0, w, axis=d) for field, w, d in zip(fields, widths, dims)]

    def pack(parts):
        return jnp.concatenate([part.reshape(-1, part.shape[-1]) for part in parts], 0)

    def unpack(flat, like):
        out, at = ([], 0)
        for part in like:
            rows = part.size // part.shape[-1]
            out.append(flat[at : at + rows].reshape(part.shape))
            at += rows
        return out

    before = unpack(lax.ppermute(pack(lasts), axis, up), lasts)
    after = unpack(lax.ppermute(pack(firsts), axis, down), firsts)
    return [
        jnp.concatenate([b, field, a], axis=d)
        for b, field, a, d in zip(before, fields, after, dims)
    ]


def z_faces(x):
    size, length = (lax.axis_size("gz"), x.shape[2])
    up = [(i, (i + 1) % size) for i in range(size)]
    down = [(j, i) for i, j in up]
    before = lax.ppermute(x[:, :, length - SPAN :], "gz", up)
    after = lax.ppermute(x[:, :, :SPAN], "gz", down)
    return jnp.concatenate([before, x, after], axis=2)


def square(operand):
    return operand * operand


def weno_value(diff_one, diff_two, diff_three, diff_four, diff_five):
    candidate_one = diff_one / 3.0 - 7.0 * diff_two / 6.0 + 11.0 * diff_three / 6.0
    candidate_two = -diff_two / 6.0 + 5.0 * diff_three / 6.0 + diff_four / 3.0
    candidate_three = diff_three / 3.0 + 5.0 * diff_four / 6.0 - diff_five / 6.0
    smooth_one = 13.0 / 12.0 * square(diff_one - 2.0 * diff_two + diff_three) + 0.25 * square(
        diff_one - 4.0 * diff_two + 3.0 * diff_three
    )
    smooth_two = 13.0 / 12.0 * square(diff_two - 2.0 * diff_three + diff_four) + 0.25 * square(
        diff_two - diff_four
    )
    smooth_three = 13.0 / 12.0 * square(diff_three - 2.0 * diff_four + diff_five) + 0.25 * square(
        3.0 * diff_three - 4.0 * diff_four + diff_five
    )
    weight_one = 0.1 / square(weno_floor + smooth_one)
    weight_two = 0.6 / square(weno_floor + smooth_two)
    weight_three = 0.3 / square(weno_floor + smooth_three)
    return (
        weight_one * candidate_one + weight_two * candidate_two + weight_three * candidate_three
    ) / (weight_one + weight_two + weight_three)


def window(padded, axis_dim, offset):
    length = padded.shape[axis_dim] - 2 * SPAN
    return lax.slice_in_dim(padded, SPAN + offset, SPAN + offset + length, axis=axis_dim)


def local_rate(padded_list, speeds):
    summed = jnp.zeros(speeds.shape[1:], jnp.float32)
    for axis_dim in range(3):
        padded = padded_list[axis_dim]
        jump_list = [
            window(padded, axis_dim, offset) - window(padded, axis_dim, offset - 1)
            for offset in range(-2, 4)
        ]
        from_left = weno_value(jump_list[0], jump_list[1], jump_list[2], jump_list[3], jump_list[4])
        from_right = weno_value(
            jump_list[5], jump_list[4], jump_list[3], jump_list[2], jump_list[1]
        )
        speed_axis = speeds[axis_dim]
        summed = (
            summed
            + jnp.maximum(speed_axis, 0.0) * from_left
            + jnp.minimum(speed_axis, 0.0) * from_right
        )
    return -summed


def shade(samples, alive, ascending):
    opacity = alive * (2.0 / CZ) / (1.0 + 4.0 * samples * samples)
    log_clear = jnp.log1p(-opacity)
    depth = jnp.arange(CZ)
    ahead = jnp.where(
        ascending, depth[:, None] < depth[None, :], depth[:, None] > depth[None, :]
    ).astype(jnp.float32)
    flat_logs = log_clear.reshape(-1, CZ)
    before = jnp.dot(flat_logs, ahead, precision=lax.Precision.HIGH).reshape(log_clear.shape)
    weight = jnp.exp(before) * opacity
    bright = jnp.tanh(samples)
    red = jnp.sum(weight * (0.5 + 0.5 * bright), -1)
    green = jnp.sum(weight * (0.5 - 0.5 * bright), -1)
    blue = jnp.sum(weight / (1.0 + samples * samples), -1)
    clear = jnp.exp(jnp.sum(log_clear, -1))
    return jnp.stack([red, green, blue, clear])


def alternate(grid_pairs):
    row_list = [jnp.stack(pixel_pair, -1) for pixel_pair in grid_pairs]
    joined = jnp.stack(row_list, -3)
    joined_shape = joined.shape
    return joined.reshape(joined_shape[:-4] + (joined_shape[-4] * 2, joined_shape[-2] * 2))


def over(front_part, back_part):
    colour = front_part[:3] + front_part[3:] * back_part[:3]
    clear = front_part[3:] * back_part[3:]
    return jnp.concatenate([colour, clear], 0)


def x_faces(x, width):
    size, length = (lax.axis_size("gx"), x.shape[0])
    up = [(i, (i + 1) % size) for i in range(size)]
    down = [(j, i) for i, j in up]
    before = lax.ppermute(x[length - width :], "gx", up)
    after = lax.ppermute(x[:width], "gx", down)
    return jnp.concatenate([before, x, after], axis=0)


def stage_rate(field, speeds):
    inner = field[:, SPAN:-SPAN]
    padded = [x_faces(inner, SPAN), field, z_faces(inner)]
    return (inner, local_rate(padded, speeds))


def shards(level_set, velocity, active_brick, depth_order):
    alive = active_brick[0, 0, 0] > 0
    alive_float = alive.astype(jnp.float32)
    flags = jnp.broadcast_to(alive_float, level_set.shape)
    stacked = jnp.stack([level_set] + [velocity[d].astype(jnp.float32) for d in range(3)] + [flags])
    halo = 3 * SPAN + 1
    stacked = exchange([stacked], "gy", [halo], 1)[0]
    level_ext = stacked[0]
    carried = stacked[1:5, :, SPAN:-SPAN]
    speed_one = carried[:3]
    speed_two = speed_one[:, :, SPAN:-SPAN]
    flag_ring = stacked[4, :, 3 * SPAN : -3 * SPAN]
    size = lax.axis_size("gx")
    up = [(i, (i + 1) % size) for i in range(size)]
    down = [(j, i) for i, j in up]
    inner = level_ext[:, SPAN:-SPAN]
    last = jnp.concatenate([inner[-SPAN:]] + [carried[c, -1:] for c in range(4)], 0)
    first = jnp.concatenate([inner[:SPAN]] + [carried[c, :1] for c in range(4)], 0)
    before = lax.ppermute(last, "gx", up)
    after = lax.ppermute(first, "gx", down)
    padded = [jnp.concatenate([before[:SPAN], inner, after[:SPAN]], 0), level_ext, z_faces(inner)]
    section_one = inner + time_step * local_rate(padded, speed_one)
    inner, rate = stage_rate(section_one, speed_two)
    section_two = 0.75 * level_ext[:, 2 * SPAN : -2 * SPAN] + 0.25 * (inner + time_step * rate)
    ring = slice(2 * SPAN, -2 * SPAN)
    edge_before = before[SPAN - 1 :, ring]
    edge_after = jnp.concatenate([after[:1], after[SPAN:]], 0)[:, ring]
    wide = x_faces(section_two, SPAN + 1)
    inner = wide[SPAN:-SPAN, SPAN:-SPAN]
    across, along, depth = (wide[:, SPAN:-SPAN], wide[SPAN:-SPAN], z_faces(inner))
    rows = inner.shape[0]

    def part(lo, hi, speeds, level, flag):
        padded = [across[lo : hi + 2 * SPAN], along[lo:hi], depth[lo:hi]]
        rate = local_rate(padded, speeds)
        advanced = level / 3.0 + 2.0 / 3.0 * (inner[lo:hi] + time_step * rate)
        return jnp.where(flag > 0, advanced, level)

    rim = jnp.concatenate(
        [
            part(0, 1, edge_before[1:4][:, None], edge_before[:1], edge_before[4:5]),
            part(
                1,
                rows - 1,
                speed_two[:, :, SPAN:-SPAN],
                level_ext[:, 3 * SPAN : -3 * SPAN],
                flag_ring,
            ),
            part(rows - 1, rows, edge_after[1:4][:, None], edge_after[:1], edge_after[4:5]),
        ],
        0,
    )
    level_out = rim[1:-1, 1:-1]
    group = lax.axis_size("gz")
    ascending = depth_order[0] < depth_order[group - 1]
    left_x = 0.75 * rim[1:-1] + 0.25 * rim[:-2]
    right_x = 0.75 * rim[1:-1] + 0.25 * rim[2:]
    grid_pairs = []
    for along_x in (left_x, right_x):
        pair_list = []
        for neighbour in (along_x[:, :-2], along_x[:, 2:]):
            samples = 0.75 * along_x[:, 1:-1] + 0.25 * neighbour
            pair_list.append(shade(samples, alive_float, ascending))
        grid_pairs.append(pair_list)
    slab_image = alternate(grid_pairs)
    rows_each = slab_image.shape[1] // group
    columns = slab_image.shape[2]
    pieces = slab_image.reshape(4, group, rows_each, columns)
    received = lax.all_to_all(pieces, "gz", split_axis=1, concat_axis=1, tiled=True)
    blended = jnp.concatenate(
        [
            jnp.zeros((3, rows_each, columns), jnp.float32),
            jnp.ones((1, rows_each, columns), jnp.float32),
        ],
        0,
    )
    for rank_value in range(group):
        chooser = (depth_order == rank_value).astype(jnp.float32)
        piece_now = jnp.einsum("s,csij->cij", chooser, received, precision=lax.Precision.HIGHEST)
        blended = over(blended, piece_now)
    image = jnp.concatenate([blended[:3], 1.0 - blended[3:]], 0)
    return (level_out, image)


def solution(mesh):
    placed = (P("gx", "gy", "gz"), P(None, "gx", "gy", "gz"), P("gx", "gy", "gz"), P())
    return jax.shard_map(
        shards,
        mesh=mesh,
        in_specs=placed,
        out_specs=(P("gx", "gy", "gz"), P(None, ("gx", "gz"), "gy")),
        check_vma=False,
    )
```

profile of v0, /device:TPU:135, one launch (start us, length us, event | category | flops | bytes accessed | tf_op | source)
XLA Modules:
  0.0 186.2 jit_solution(2061402217357418076)
XLA Ops:
  1.4 1.1 bitcast_dynamic-update-slice_fusion
  2.4 1.0 convert_dynamic-update-slice_fusion.2
  4.1 4.6 %collective-permute-start.1 = (f32[5,32,10,128]{3,1,2,0:T(8,128)S(1)}, f32[5,32,10,128]{3,1,2,0:T(8,128)S(1)}, u32[]{:S(2)}, u32[]{:S(2)}) collective-permute-start(f32[5,32,10,128]{3,1,2,0:T(8,128)S(1)} %copy.8), channel_id=1, source_target_pairs={{4,0},{8,4},{12,8},{0,12},{5,1},{9,5},{13,9},{1,13},{6,2},{10,6},{... | collective-permute-start | bytes 2457608 | tf_op jit(solution)/shard_map/ppermute | solution.py:22
  9.0 1.9 %collective-permute-start = (f32[5,32,10,128]{3,1,2,0:T(8,128)S(1)}, f32[5,32,10,128]{3,1,2,0:T(8,128)S(1)}, u32[]{:S(2)}, u32[]{:S(2)}) collective-permute-start(f32[5,32,10,128]{3,1,2,0:T(8,128)S(1)} %copy.7), channel_id=1, source_target_pairs={{0,4},{4,8},{8,12},{12,0},{1,5},{5,9},{9,13},{13,1},{2,6},{6,10},{... | collective-permute-start | bytes 2457608 | tf_op jit(solution)/shard_map/ppermute | solution.py:21
  11.0 14.7 %collective-permute-done.1 = f32[5,32,10,128]{3,1,2,0:T(8,128)S(1)} collective-permute-done((f32[5,32,10,128]{3,1,2,0:T(8,128)S(1)}, f32[5,32,10,128]{3,1,2,0:T(8,128)S(1)}, u32[]{:S(2)}, u32[]{:S(2)}) %collective-permute-start.1) | collective-permute-done | bytes 819232 | tf_op jit(solution)/shard_map/ppermute | solution.py:22
  26.2 4.8 %collective-permute-done = f32[5,32,10,128]{3,1,2,0:T(8,128)S(1)} collective-permute-done((f32[5,32,10,128]{3,1,2,0:T(8,128)S(1)}, f32[5,32,10,128]{3,1,2,0:T(8,128)S(1)}, u32[]{:S(2)}, u32[]{:S(2)}) %collective-permute-start) | collective-permute-done | bytes 819232 | tf_op jit(solution)/shard_map/ppermute | solution.py:21
  32.1 0.8 slice_dynamic-update-slice_fusion
  32.9 1.1 constant_dynamic-update-slice_fusion.7
  34.2 0.6 constant_dynamic-update-slice_fusion.6
  36.0 10.4 %collective-permute-start.2 = (f32[7,46,128]{2,1,0:T(8,128)}, f32[7,46,128]{2,1,0:T(8,128)S(1)}, u32[]{:S(2)}, u32[]{:S(2)}) collective-permute-start(f32[7,46,128]{2,1,0:T(8,128)} %get-tuple-element.19), channel_id=1, source_target_pairs={{0,16},{16,32},{32,48},{48,64},{64,80},{80,96},{96,112},{112,128},... | collective-permute-start | bytes 494600 | tf_op jit(solution)/shard_map/ppermute | solution.py:181
  46.4 1.9 %collective-permute-start.3 = (f32[7,46,128]{2,1,0:T(8,128)}, f32[7,46,128]{2,1,0:T(8,128)}, u32[]{:S(2)}, u32[]{:S(2)}) collective-permute-start(f32[7,46,128]{2,1,0:T(8,128)} %get-tuple-element.18), channel_id=1, source_target_pairs={{16,0},{32,16},{48,32},{64,48},{80,64},{96,80},{112,96},{128,112},... | collective-permute-start | bytes 494600 | tf_op jit(solution)/shard_map/ppermute | solution.py:182
  49.0 2.6 %collective-permute-start.4 = (f32[32,46,3]{1,0,2:T(8,128)S(1)}, f32[32,46,3]{1,0,2:T(8,128)S(1)}, u32[]{:S(2)}, u32[]{:S(2)}) collective-permute-start(f32[32,46,3]{1,0,2:T(8,128)S(1)} %copy.11), channel_id=1, source_target_pairs={{0,1},{1,2},{2,3},{3,0},{4,5},{5,6},{6,7},{7,4},{8,9},{9,10},{10,1... | collective-permute-start | bytes 53000 | tf_op jit(solution)/shard_map/ppermute | solution.py:61
  52.0 4.4 %collective-permute-start.5 = (f32[32,46,3]{1,0,2:T(8,128)S(1)}, f32[32,46,3]{1,0,2:T(8,128)S(1)}, u32[]{:S(2)}, u32[]{:S(2)}) collective-permute-start(f32[32,46,3]{1,0,2:T(8,128)S(1)} %copy.13), channel_id=1, source_target_pairs={{1,0},{2,1},{3,2},{0,3},{5,4},{6,5},{7,6},{4,7},{9,8},{10,9},{11,1... | collective-permute-start | bytes 53000 | tf_op jit(solution)/shard_map/ppermute | solution.py:62
  56.5 1.3 copy.12
  57.8 1.3 copy.14
  59.1 3.0 %collective-permute-done.3 = f32[7,46,128]{2,1,0:T(8,128)} collective-permute-done((f32[7,46,128]{2,1,0:T(8,128)}, f32[7,46,128]{2,1,0:T(8,128)}, u32[]{:S(2)}, u32[]{:S(2)}) %collective-permute-start.3) | collective-permute-done | bytes 164896 | tf_op jit(solution)/shard_map/ppermute | solution.py:182
  62.1 0.9 slice.985
  63.0 15.0 %fusion.21 = f32[32,46,128]{2,1,0:T(8,128)S(1)} fusion(f32[32,46,128]{2,1,0:T(8,128)S(1)} %slice.976, f32[32,46,3]{2,1,0:T(8,128)} %copy.14, f32[32,46,3]{2,1,0:T(8,128)} %copy.12, f32[5,32,52,128]{3,2,1,0:T(8,128)} %copy-done, f32[32,52,128]{2,1,0:T(8,128)S(1)} %slice_bitcast_fusion, f32[3,46,128]{2,1,0:T(8,128)S(1)} %slice.979, f32[3,46,128]{2,1,0:T(8,128)S(1)} %slice.985), kind=kLoop, calls=%fused_computation.99 | loop fusion | flops 79511552 | bytes 8466944 | tf_op jit(solution)/shard_map/add | solution.py:184
  78.0 10.1 %collective-permute-start.6 = (f32[3,40,128]{2,1,0:T(8,128)S(1)}, f32[3,40,128]{2,1,0:T(8,128)S(1)}, u32[]{:S(2)}, u32[]{:S(2)}) collective-permute-start(f32[3,40,128]{2,1,0:T(8,128)S(1)} %get-tuple-element.35), channel_id=1, source_target_pairs={{0,16},{16,32},{32,48},{48,64},{64,80},{80,96},{96,112},{112,128},... | collective-permute-start | bytes 184328 | tf_op jit(solution)/shard_map/ppermute | solution.py:152
  88.2 1.9 %collective-permute-start.7 = (f32[3,40,128]{2,1,0:T(8,128)S(1)}, f32[3,40,128]{2,1,0:T(8,128)S(1)}, u32[]{:S(2)}, u32[]{:S(2)}) collective-permute-start(f32[3,40,128]{2,1,0:T(8,128)S(1)} %get-tuple-element.34), channel_id=1, source_target_pairs={{16,0},{32,16},{48,32},{64,48},{80,64},{96,80},{112,96},{128,112},... | collective-permute-start | bytes 184328 | tf_op jit(solution)/shard_map/ppermute | solution.py:153
  90.6 1.9 %collective-permute-start.8 = (f32[32,40,3]{1,0,2:T(8,128)S(1)}, f32[32,40,3]{1,0,2:T(8,128)S(1)}, u32[]{:S(2)}, u32[]{:S(2)}) collective-permute-start(f32[32,40,3]{1,0,2:T(8,128)S(1)} %copy.15), channel_id=1, source_target_pairs={{0,1},{1,2},{2,3},{3,0},{4,5},{5,6},{6,7},{7,4},{8,9},{9,10},{10,1... | collective-permute-start | bytes 46088 | tf_op jit(solution)/shard_map/ppermute | solution.py:61
  92.6 0.9 copy.17
  93.5 5.1 %collective-permute-start.9 = (f32[32,40,3]{1,0,2:T(8,128)}, f32[32,40,3]{1,0,2:T(8,128)S(1)}, u32[]{:S(2)}, u32[]{:S(2)}) collective-permute-start(f32[32,40,3]{1,0,2:T(8,128)} %copy.17), channel_id=1, source_target_pairs={{1,0},{2,1},{3,2},{0,3},{5,4},{6,5},{7,6},{4,7},{9,8},{10,9},{11,1... | collective-permute-start | bytes 46088 | tf_op jit(solution)/shard_map/ppermute | solution.py:62
  98.7 1.2 copy.16
  100.1 1.2 copy.18
  101.3 13.0 %fusion.174 = f32[32,40,128]{2,1,0:T(8,128)S(1)} fusion(f32[32,52,128]{2,1,0:T(8,128)S(1)} %slice_bitcast_fusion, f32[32,40,128]{2,1,0:T(8,128)S(1)} %slice.1008, f32[32,40,3]{2,1,0:T(8,128)} %copy.18, f32[32,40,3]{2,1,0:T(8,128)} %copy.16, f32[5,32,52,128]{3,2,1,0:T(8,128)} %copy-done, f32[32,46,128]{2,1,0:T(8,128)S(1)} %fusion.21, ...), kind=kLoop, calls=%fused_computation.299 | loop fusion | flops 69632000 | bytes 8017920 | tf_op jit(solution)/shard_map/add | solution.py:186
  114.3 10.8 %collective-permute-start.10 = (f32[4,40,128]{2,1,0:T(8,128)S(1)}, f32[4,40,128]{2,1,0:T(8,128)S(1)}, u32[]{:S(2)}, u32[]{:S(2)}) collective-permute-start(f32[4,40,128]{2,1,0:T(8,128)S(1)} %get-tuple-element.44), channel_id=1, source_target_pairs={{0,16},{16,32},{32,48},{48,64},{64,80},{80,96},{96,112},{112,128},... | collective-permute-start | bytes 245768 | tf_op jit(solution)/shard_map/ppermute | solution.py:152
  125.1 1.9 %collective-permute-start.11 = (f32[4,40,128]{2,1,0:T(8,128)S(1)}, f32[4,40,128]{2,1,0:T(8,128)S(1)}, u32[]{:S(2)}, u32[]{:S(2)}) collective-permute-start(f32[4,40,128]{2,1,0:T(8,128)S(1)} %get-tuple-element.45), channel_id=1, source_target_pairs={{16,0},{32,16},{48,32},{64,48},{80,64},{96,80},{112,96},{128,112},... | collective-permute-start | bytes 245768 | tf_op jit(solution)/shard_map/ppermute | solution.py:153
  127.2 10.0 %collective-permute-done.11 = f32[4,40,128]{2,1,0:T(8,128)S(1)} collective-permute-done((f32[4,40,128]{2,1,0:T(8,128)S(1)}, f32[4,40,128]{2,1,0:T(8,128)S(1)}, u32[]{:S(2)}, u32[]{:S(2)}) %collective-permute-start.11) | collective-permute-done | bytes 81952 | tf_op jit(solution)/shard_map/ppermute | solution.py:153
  137.2 1.1 fusion.456
  138.3 1.5 copy.19
  139.8 1.9 %collective-permute-start.12 = (f32[34,34,3]{1,0,2:T(8,128)S(1)}, f32[34,34,3]{1,0,2:T(8,128)S(1)}, u32[]{:S(2)}, u32[]{:S(2)}) collective-permute-start(f32[34,34,3]{1,0,2:T(8,128)S(1)} %copy.19), channel_id=1, source_target_pairs={{0,1},{1,2},{2,3},{3,0},{4,5},{5,6},{6,7},{7,4},{8,9},{9,10},{10,1... | collective-permute-start | bytes 41624 | tf_op jit(solution)/shard_map/ppermute | solution.py:61
  141.7 1.0 copy.21
  142.7 5.8 %collective-permute-start.13 = (f32[34,34,3]{1,0,2:T(8,128)}, f32[34,34,3]{1,0,2:T(8,128)S(1)}, u32[]{:S(2)}, u32[]{:S(2)}) collective-permute-start(f32[34,34,3]{1,0,2:T(8,128)} %copy.21), channel_id=1, source_target_pairs={{1,0},{2,1},{3,2},{0,3},{5,4},{6,5},{7,6},{4,7},{9,8},{10,9},{11,1... | collective-permute-start | bytes 41624 | tf_op jit(solution)/shard_map/ppermute | solution.py:62
  150.3 0.9 slice.1059
  152.0 1.5 add_select_fusion
  153.8 13.2 %fusion.181 = f32[32,34,128]{2,1,0:T(8,128)S(1)} fusion(f32[34,34,3]{2,1,0:T(8,128)S(1)} %copy.22, f32[34,34,128]{2,1,0:T(8,128)S(1)} %copy-done.1, f32[34,34,3]{2,1,0:T(8,128)S(1)} %copy.20, f32[5,32,52,128]{3,2,1,0:T(8,128)} %copy-done, f32[32,40,128]{2,1,0:T(8,128)S(1)} %fusion.174, f32[4,40,128]{2,1,0:T(8,128)S(1)} %collective-permute-done.11, ...), kind=kLoop, calls=%fused_computation.308 | loop fusion | flops 59465728 | bytes 10936320 | tf_op jit(solution)/shard_map/jit(_where)/select_n | solution.py:199
  167.9 1.0 multiply_reduce_fusion.7
  168.9 1.0 multiply_reduce_fusion.5
  170.0 1.0 multiply_reduce_fusion.3
  171.0 1.0 multiply_reduce_fusion.1
  172.2 1.3 copy.23
  173.5 0.7 copy.24
  174.2 0.8 reshape.120
  175.0 3.3 %all-to-all-start = ((f32[4,1,4096]{2,1,0:T(1,128)}), f32[4,1,4096]{2,1,0:T(1,128)S(1)}, u32[]{:S(2)}, u32[]{:S(2)}) async-start(f32[4,1,4096]{2,1,0:T(1,128)} %reshape.120), calls=%async_computation | async-start | bytes 131072 | tf_op jit(solution)/shard_map/all_to_all | solution.py:231
  178.3 0.9 slice.1073
  179.1 3.7 %all-to-all-done = f32[4,1,4096]{2,1,0:T(1,128)S(1)} async-done(((f32[4,1,4096]{2,1,0:T(1,128)}), f32[4,1,4096]{2,1,0:T(1,128)S(1)}, u32[]{:S(2)}, u32[]{:S(2)}) %all-to-all-start) | async-done | bytes 65568 | tf_op jit(solution)/shard_map/all_to_all | solution.py:231
  183.3 0.8 reduce
  (71 shorter events, 11.1 us)
Async XLA Ops:
  0.6 2.8 %copy-start.4 = (bf16[3,32,32,128]{3,2,1,0:T(8,128)(2,1)S(1)}, bf16[3,32,32,128]{3,2,1,0:T(8,128)(2,1)}, u32[]{:S(2)}) copy-start(bf16[3,32,32,128]{3,2,1,0:T(8,128)(2,1)} %param.5) | copy-start | bytes 2359300
  4.1 21.6 %collective-permute-start.1 = (f32[5,32,10,128]{3,1,2,0:T(8,128)S(1)}, f32[5,32,10,128]{3,1,2,0:T(8,128)S(1)}, u32[]{:S(2)}, u32[]{:S(2)}) collective-permute-start(f32[5,32,10,128]{3,1,2,0:T(8,128)S(1)} %copy.8), channel_id=1, source_target_pairs={{4,0},{8,4},{12,8},{0,12},{5,1},{9,5},{13,9},{1,13},{6,2},{10,6},{... | collective-permute-start | bytes 2457608 | tf_op jit(solution)/shard_map/ppermute | solution.py:22
  9.0 22.0 %collective-permute-start = (f32[5,32,10,128]{3,1,2,0:T(8,128)S(1)}, f32[5,32,10,128]{3,1,2,0:T(8,128)S(1)}, u32[]{:S(2)}, u32[]{:S(2)}) collective-permute-start(f32[5,32,10,128]{3,1,2,0:T(8,128)S(1)} %copy.7), channel_id=1, source_target_pairs={{0,4},{4,8},{8,12},{12,0},{1,5},{5,9},{9,13},{13,1},{2,6},{6,10},{... | collective-permute-start | bytes 2457608 | tf_op jit(solution)/shard_map/ppermute | solution.py:21
  32.0 2.1 %copy-start = (f32[5,32,52,128]{3,2,1,0:T(8,128)}, f32[5,32,52,128]{3,2,1,0:T(8,128)S(1)}, u32[]{:S(2)}) copy-start(f32[5,32,52,128]{3,2,1,0:T(8,128)S(1)} %pad_maximum_fusion) | copy-start | bytes 12779524
  36.0 23.0 %collective-permute-start.2 = (f32[7,46,128]{2,1,0:T(8,128)}, f32[7,46,128]{2,1,0:T(8,128)S(1)}, u32[]{:S(2)}, u32[]{:S(2)}) collective-permute-start(f32[7,46,128]{2,1,0:T(8,128)} %get-tuple-element.19), channel_id=1, source_target_pairs={{0,16},{16,32},{32,48},{48,64},{64,80},{80,96},{96,112},{112,128},... | collective-permute-start | bytes 494600 | tf_op jit(solution)/shard_map/ppermute | solution.py:181
  46.4 15.7 %collective-permute-start.3 = (f32[7,46,128]{2,1,0:T(8,128)}, f32[7,46,128]{2,1,0:T(8,128)}, u32[]{:S(2)}, u32[]{:S(2)}) collective-permute-start(f32[7,46,128]{2,1,0:T(8,128)} %get-tuple-element.18), channel_id=1, source_target_pairs={{16,0},{32,16},{48,32},{64,48},{80,64},{96,80},{112,96},{128,112},... | collective-permute-start | bytes 494600 | tf_op jit(solution)/shard_map/ppermute | solution.py:182
  49.0 7.5 %collective-permute-start.4 = (f32[32,46,3]{1,0,2:T(8,128)S(1)}, f32[32,46,3]{1,0,2:T(8,128)S(1)}, u32[]{:S(2)}, u32[]{:S(2)}) collective-permute-start(f32[32,46,3]{1,0,2:T(8,128)S(1)} %copy.11), channel_id=1, source_target_pairs={{0,1},{1,2},{2,3},{3,0},{4,5},{5,6},{6,7},{7,4},{8,9},{9,10},{10,1... | collective-permute-start | bytes 53000 | tf_op jit(solution)/shard_map/ppermute | solution.py:61
  52.0 5.8 %collective-permute-start.5 = (f32[32,46,3]{1,0,2:T(8,128)S(1)}, f32[32,46,3]{1,0,2:T(8,128)S(1)}, u32[]{:S(2)}, u32[]{:S(2)}) collective-permute-start(f32[32,46,3]{1,0,2:T(8,128)S(1)} %copy.13), channel_id=1, source_target_pairs={{1,0},{2,1},{3,2},{0,3},{5,4},{6,5},{7,6},{4,7},{9,8},{10,9},{11,1... | collective-permute-start | bytes 53000 | tf_op jit(solution)/shard_map/ppermute | solution.py:62
  78.0 23.2 %collective-permute-start.6 = (f32[3,40,128]{2,1,0:T(8,128)S(1)}, f32[3,40,128]{2,1,0:T(8,128)S(1)}, u32[]{:S(2)}, u32[]{:S(2)}) collective-permute-start(f32[3,40,128]{2,1,0:T(8,128)S(1)} %get-tuple-element.35), channel_id=1, source_target_pairs={{0,16},{16,32},{32,48},{48,64},{64,80},{80,96},{96,112},{112,128},... | collective-permute-start | bytes 184328 | tf_op jit(solution)/shard_map/ppermute | solution.py:152
  88.2 13.1 %collective-permute-start.7 = (f32[3,40,128]{2,1,0:T(8,128)S(1)}, f32[3,40,128]{2,1,0:T(8,128)S(1)}, u32[]{:S(2)}, u32[]{:S(2)}) collective-permute-start(f32[3,40,128]{2,1,0:T(8,128)S(1)} %get-tuple-element.34), channel_id=1, source_target_pairs={{16,0},{32,16},{48,32},{64,48},{80,64},{96,80},{112,96},{128,112},... | collective-permute-start | bytes 184328 | tf_op jit(solution)/shard_map/ppermute | solution.py:153
  90.6 8.1 %collective-permute-start.8 = (f32[32,40,3]{1,0,2:T(8,128)S(1)}, f32[32,40,3]{1,0,2:T(8,128)S(1)}, u32[]{:S(2)}, u32[]{:S(2)}) collective-permute-start(f32[32,40,3]{1,0,2:T(8,128)S(1)} %copy.15), channel_id=1, source_target_pairs={{0,1},{1,2},{2,3},{3,0},{4,5},{5,6},{6,7},{7,4},{8,9},{9,10},{10,1... | collective-permute-start | bytes 46088 | tf_op jit(solution)/shard_map/ppermute | solution.py:61
  93.5 6.6 %collective-permute-start.9 = (f32[32,40,3]{1,0,2:T(8,128)}, f32[32,40,3]{1,0,2:T(8,128)S(1)}, u32[]{:S(2)}, u32[]{:S(2)}) collective-permute-start(f32[32,40,3]{1,0,2:T(8,128)} %copy.17), channel_id=1, source_target_pairs={{1,0},{2,1},{3,2},{0,3},{5,4},{6,5},{7,6},{4,7},{9,8},{10,9},{11,1... | collective-permute-start | bytes 46088 | tf_op jit(solution)/shard_map/ppermute | solution.py:62
  114.3 12.8 %collective-permute-start.10 = (f32[4,40,128]{2,1,0:T(8,128)S(1)}, f32[4,40,128]{2,1,0:T(8,128)S(1)}, u32[]{:S(2)}, u32[]{:S(2)}) collective-permute-start(f32[4,40,128]{2,1,0:T(8,128)S(1)} %get-tuple-element.44), channel_id=1, source_target_pairs={{0,16},{16,32},{32,48},{48,64},{64,80},{80,96},{96,112},{112,128},... | collective-permute-start | bytes 245768 | tf_op jit(solution)/shard_map/ppermute | solution.py:152
  125.1 12.0 %collective-permute-start.11 = (f32[4,40,128]{2,1,0:T(8,128)S(1)}, f32[4,40,128]{2,1,0:T(8,128)S(1)}, u32[]{:S(2)}, u32[]{:S(2)}) collective-permute-start(f32[4,40,128]{2,1,0:T(8,128)S(1)} %get-tuple-element.45), channel_id=1, source_target_pairs={{16,0},{32,16},{48,32},{64,48},{80,64},{96,80},{112,96},{128,112},... | collective-permute-start | bytes 245768 | tf_op jit(solution)/shard_map/ppermute | solution.py:153
  137.2 11.3 %copy-start.5 = (s32[4]{0:T(128)S(1)}, s32[4]{0:T(128)}, u32[]{:S(2)}) copy-start(s32[4]{0:T(128)} %param.7) | copy-start | bytes 52
  139.8 11.5 %collective-permute-start.12 = (f32[34,34,3]{1,0,2:T(8,128)S(1)}, f32[34,34,3]{1,0,2:T(8,128)S(1)}, u32[]{:S(2)}, u32[]{:S(2)}) collective-permute-start(f32[34,34,3]{1,0,2:T(8,128)S(1)} %copy.19), channel_id=1, source_target_pairs={{0,1},{1,2},{2,3},{3,0},{4,5},{5,6},{6,7},{7,4},{8,9},{9,10},{10,1... | collective-permute-start | bytes 41624 | tf_op jit(solution)/shard_map/ppermute | solution.py:61
  142.7 8.9 %collective-permute-start.13 = (f32[34,34,3]{1,0,2:T(8,128)}, f32[34,34,3]{1,0,2:T(8,128)S(1)}, u32[]{:S(2)}, u32[]{:S(2)}) collective-permute-start(f32[34,34,3]{1,0,2:T(8,128)} %copy.21), channel_id=1, source_target_pairs={{1,0},{2,1},{3,2},{0,3},{5,4},{6,5},{7,6},{4,7},{9,8},{10,9},{11,1... | collective-permute-start | bytes 41624 | tf_op jit(solution)/shard_map/ppermute | solution.py:62
  152.0 1.5 copy-start.1
  167.1 0.8 copy-start.2
  173.5 4.7 %copy-start.3 = (f32[32,34,128]{2,1,0:T(8,128)S(1)}, f32[32,34,128]{2,1,0:T(8,128)}, u32[]{:S(2)}) copy-start(f32[32,34,128]{2,1,0:T(8,128)} %copy-done.2) | copy-start | bytes 1671172
  175.0 7.9 %all-to-all-start = ((f32[4,1,4096]{2,1,0:T(1,128)}), f32[4,1,4096]{2,1,0:T(1,128)S(1)}, u32[]{:S(2)}, u32[]{:S(2)}) async-start(f32[4,1,4096]{2,1,0:T(1,128)} %reshape.120), calls=%async_computation | async-start | bytes 131072 | tf_op jit(solution)/shard_map/all_to_all | solution.py:231
where the time goes:
time: 187 us; the launch traced here: 186 us
  starting transfers between devices  68.8 us (37%)
  other arithmetic  49.7 us (27%)
  waiting for transfers between devices  36.6 us (20%)
  local copies, waits for them, and re-layouts  22.6 us (12%)
  matrix products  5.36 us (3%)
  between operations  3.14 us (2%)
    ppermute x2, starting transfers between devices, x_faces(): before = lax.ppermute(x[length - width:], 'gx', up)  20.9 us
    ppermute x3, starting transfers between devices, z_faces(): after = lax.ppermute(x[:, :, :SPAN], 'gz', down)  15.4 us
    select_n x3, other arithmetic, part(): return jnp.where(flag > 0, advanced, level)  15.1 us
    add x1, other arithmetic, shards(): section_one = inner + time_step * local_rate(padded, speed_one)  15 us
    ppermute x1, waiting for transfers between devices, exchange(): after = lax.ppermute(first, axis, down)  14.7 us
    add x1, other arithmetic, shards(): 0.75 * level_ext[:, 2 * SPAN:-2 * SPAN] + 0.25 * (inner + time_step * rate)  13 us
    ppermute x1, starting transfers between devices, shards(): before = lax.ppermute(last, 'gx', up)  10.4 us
    ppermute x2, waiting for transfers between devices, x_faces(): after = lax.ppermute(x[:width], 'gx', down)  9.96 us
  transfers between devices with their start and end apart: 15, of which 7 were waited for; matrix products, arithmetic and copies ran while one was open for 6% of the time, Pallas kernels for 0%

commit v1 on v0

--- a/solution.py
+++ b/solution.py
@@ -228,7 +228,10 @@
     rows_each = slab_image.shape[1] // group
     columns = slab_image.shape[2]
     pieces = slab_image.reshape(4, group, rows_each, columns)
-    received = lax.all_to_all(pieces, "gz", split_axis=1, concat_axis=1, tiled=True)
+    received = jnp.concatenate(
+        lax.all_to_all(jnp.stack(jnp.split(pieces, lax.axis_size("gz"), axis=1)), "gz", 0, 0),
+        axis=1,
+    )
     blended = jnp.concatenate(
         [
             jnp.zeros((3, rows_each, columns), jnp.float32),

time: 187 us -> 188 us (level)
  the two profiles are of different devices: /device:TPU:135 before, /device:TPU:143 now
where the time goes in v1:
time: 188 us; the launch traced here: 187 us
  starting transfers between devices  67.6 us (36%)
  other arithmetic  49.8 us (26%)
  waiting for transfers between devices  35.2 us (19%)
  local copies, waits for them, and re-layouts  26 us (14%)
  matrix products  5.36 us (3%)
  between operations  3.15 us (2%)
    ppermute x2, starting transfers between devices, x_faces(): before = lax.ppermute(x[length - width:], 'gx', up)  20.9 us
    ppermute x1, waiting for transfers between devices, exchange(): before = lax.ppermute(last, axis, up)  15.5 us
    ppermute x3, starting transfers between devices, z_faces(): after = lax.ppermute(x[:, :, :SPAN], 'gz', down)  15.4 us
    select_n x3, other arithmetic, part(): return jnp.where(flag > 0, advanced, level)  15.1 us
    add x1, other arithmetic, shards(): section_one = inner + time_step * local_rate(padded, speed_one)  15 us
    add x1, other arithmetic, shards(): 0.75 * level_ext[:, 2 * SPAN:-2 * SPAN] + 0.25 * (inner + time_step * rate)  13 us
    ppermute x1, starting transfers between devices, shards(): before = lax.ppermute(last, 'gx', up)  10.4 us
    ppermute x2, waiting for transfers between devices, x_faces(): after = lax.ppermute(x[:width], 'gx', down)  9.96 us
  transfers between devices with their start and end apart: 15, of which 7 were waited for; matrix products, arithmetic and copies ran while one was open for 6% of the time, Pallas kernels for 0%

profile of v1, /device:TPU:143, one launch (start us, length us, event | category | flops | bytes accessed | tf_op | source)
XLA Modules:
  0.0 187.1 jit_solution(18389613495031028751)
XLA Ops:
  1.4 1.1 bitcast_dynamic-update-slice_fusion
  2.4 1.0 convert_dynamic-update-slice_fusion.2
  4.1 3.2 %collective-permute-start = (f32[5,32,10,128]{3,1,2,0:T(8,128)S(1)}, f32[5,32,10,128]{3,1,2,0:T(8,128)S(1)}, u32[]{:S(2)}, u32[]{:S(2)}) collective-permute-start(f32[5,32,10,128]{3,1,2,0:T(8,128)S(1)} %copy.10), channel_id=1, source_target_pairs={{0,4},{4,8},{8,12},{12,0},{1,5},{5,9},{9,13},{13,1},{2,6},{6,10},{... | collective-permute-start | bytes 2457608 | tf_op jit(solution)/shard_map/ppermute | solution.py:21
  7.6 2.1 %collective-permute-start.1 = (f32[5,32,10,128]{3,1,2,0:T(8,128)S(1)}, f32[5,32,10,128]{3,1,2,0:T(8,128)S(1)}, u32[]{:S(2)}, u32[]{:S(2)}) collective-permute-start(f32[5,32,10,128]{3,1,2,0:T(8,128)S(1)} %copy.11), channel_id=1, source_target_pairs={{4,0},{8,4},{12,8},{0,12},{5,1},{9,5},{13,9},{1,13},{6,2},{10,6},{... | collective-permute-start | bytes 2457608 | tf_op jit(solution)/shard_map/ppermute | solution.py:22
  9.7 15.5 %collective-permute-done = f32[5,32,10,128]{3,1,2,0:T(8,128)S(1)} collective-permute-done((f32[5,32,10,128]{3,1,2,0:T(8,128)S(1)}, f32[5,32,10,128]{3,1,2,0:T(8,128)S(1)}, u32[]{:S(2)}, u32[]{:S(2)}) %collective-permute-start) | collective-permute-done | bytes 819232 | tf_op jit(solution)/shard_map/ppermute | solution.py:21
  25.6 2.7 %collective-permute-done.1 = f32[5,32,10,128]{3,1,2,0:T(8,128)S(1)} collective-permute-done((f32[5,32,10,128]{3,1,2,0:T(8,128)S(1)}, f32[5,32,10,128]{3,1,2,0:T(8,128)S(1)}, u32[]{:S(2)}, u32[]{:S(2)}) %collective-permute-start.1) | collective-permute-done | bytes 819232 | tf_op jit(solution)/shard_map/ppermute | solution.py:22
  29.5 0.8 slice_dynamic-update-slice_fusion
  30.2 1.1 constant_dynamic-update-slice_fusion.7
  33.4 10.4 %collective-permute-start.2 = (f32[7,46,128]{2,1,0:T(8,128)}, f32[7,46,128]{2,1,0:T(8,128)S(1)}, u32[]{:S(2)}, u32[]{:S(2)}) collective-permute-start(f32[7,46,128]{2,1,0:T(8,128)} %get-tuple-element.19), channel_id=1, source_target_pairs={{0,16},{16,32},{32,48},{48,64},{64,80},{80,96},{96,112},{112,128},... | collective-permute-start | bytes 494600 | tf_op jit(solution)/shard_map/ppermute | solution.py:181
  43.8 1.9 %collective-permute-start.3 = (f32[7,46,128]{2,1,0:T(8,128)}, f32[7,46,128]{2,1,0:T(8,128)}, u32[]{:S(2)}, u32[]{:S(2)}) collective-permute-start(f32[7,46,128]{2,1,0:T(8,128)} %get-tuple-element.18), channel_id=1, source_target_pairs={{16,0},{32,16},{48,32},{64,48},{80,64},{96,80},{112,96},{128,112},... | collective-permute-start | bytes 494600 | tf_op jit(solution)/shard_map/ppermute | solution.py:182
  46.4 2.6 %collective-permute-start.4 = (f32[32,46,3]{1,0,2:T(8,128)S(1)}, f32[32,46,3]{1,0,2:T(8,128)S(1)}, u32[]{:S(2)}, u32[]{:S(2)}) collective-permute-start(f32[32,46,3]{1,0,2:T(8,128)S(1)} %copy.14), channel_id=1, source_target_pairs={{0,1},{1,2},{2,3},{3,0},{4,5},{5,6},{6,7},{7,4},{8,9},{9,10},{10,1... | collective-permute-start | bytes 53000 | tf_op jit(solution)/shard_map/ppermute | solution.py:61
  49.4 4.4 %collective-permute-start.5 = (f32[32,46,3]{1,0,2:T(8,128)S(1)}, f32[32,46,3]{1,0,2:T(8,128)S(1)}, u32[]{:S(2)}, u32[]{:S(2)}) collective-permute-start(f32[32,46,3]{1,0,2:T(8,128)S(1)} %copy.16), channel_id=1, source_target_pairs={{1,0},{2,1},{3,2},{0,3},{5,4},{6,5},{7,6},{4,7},{9,8},{10,9},{11,1... | collective-permute-start | bytes 53000 | tf_op jit(solution)/shard_map/ppermute | solution.py:62
  53.9 1.3 copy.15
  55.2 1.3 copy.17
  56.4 3.0 %collective-permute-done.3 = f32[7,46,128]{2,1,0:T(8,128)} collective-permute-done((f32[7,46,128]{2,1,0:T(8,128)}, f32[7,46,128]{2,1,0:T(8,128)}, u32[]{:S(2)}, u32[]{:S(2)}) %collective-permute-start.3) | collective-permute-done | bytes 164896 | tf_op jit(solution)/shard_map/ppermute | solution.py:182
  59.5 0.9 slice.985
  60.4 15.0 %fusion.21 = f32[32,46,128]{2,1,0:T(8,128)S(1)} fusion(f32[32,46,128]{2,1,0:T(8,128)S(1)} %slice.976, f32[32,46,3]{2,1,0:T(8,128)} %copy.17, f32[32,46,3]{2,1,0:T(8,128)} %copy.15, f32[5,32,52,128]{3,2,1,0:T(8,128)} %copy-done, f32[32,52,128]{2,1,0:T(8,128)S(1)} %slice_bitcast_fusion, f32[3,46,128]{2,1,0:T(8,128)S(1)} %slice.979, f32[3,46,128]{2,1,0:T(8,128)S(1)} %slice.985), kind=kLoop, calls=%fused_computation.99 | loop fusion | flops 79511552 | bytes 8466944 | tf_op jit(solution)/shard_map/add | solution.py:184
  75.4 10.1 %collective-permute-start.6 = (f32[3,40,128]{2,1,0:T(8,128)S(1)}, f32[3,40,128]{2,1,0:T(8,128)S(1)}, u32[]{:S(2)}, u32[]{:S(2)}) collective-permute-start(f32[3,40,128]{2,1,0:T(8,128)S(1)} %get-tuple-element.39), channel_id=1, source_target_pairs={{0,16},{16,32},{32,48},{48,64},{64,80},{80,96},{96,112},{112,128},... | collective-permute-start | bytes 184328 | tf_op jit(solution)/shard_map/ppermute | solution.py:152
  85.5 1.9 %collective-permute-start.7 = (f32[3,40,128]{2,1,0:T(8,128)S(1)}, f32[3,40,128]{2,1,0:T(8,128)S(1)}, u32[]{:S(2)}, u32[]{:S(2)}) collective-permute-start(f32[3,40,128]{2,1,0:T(8,128)S(1)} %get-tuple-element.38), channel_id=1, source_target_pairs={{16,0},{32,16},{48,32},{64,48},{80,64},{96,80},{112,96},{128,112},... | collective-permute-start | bytes 184328 | tf_op jit(solution)/shard_map/ppermute | solution.py:153
  88.0 1.9 %collective-permute-start.8 = (f32[32,40,3]{1,0,2:T(8,128)S(1)}, f32[32,40,3]{1,0,2:T(8,128)S(1)}, u32[]{:S(2)}, u32[]{:S(2)}) collective-permute-start(f32[32,40,3]{1,0,2:T(8,128)S(1)} %copy.18), channel_id=1, source_target_pairs={{0,1},{1,2},{2,3},{3,0},{4,5},{5,6},{6,7},{7,4},{8,9},{9,10},{10,1... | collective-permute-start | bytes 46088 | tf_op jit(solution)/shard_map/ppermute | solution.py:61
  89.9 0.9 copy.20
  90.8 5.1 %collective-permute-start.9 = (f32[32,40,3]{1,0,2:T(8,128)}, f32[32,40,3]{1,0,2:T(8,128)S(1)}, u32[]{:S(2)}, u32[]{:S(2)}) collective-permute-start(f32[32,40,3]{1,0,2:T(8,128)} %copy.20), channel_id=1, source_target_pairs={{1,0},{2,1},{3,2},{0,3},{5,4},{6,5},{7,6},{4,7},{9,8},{10,9},{11,1... | collective-permute-start | bytes 46088 | tf_op jit(solution)/shard_map/ppermute | solution.py:62
  96.1 1.2 copy.19
  97.5 1.2 copy.21
  98.6 13.0 %fusion.174 = f32[32,40,128]{2,1,0:T(8,128)S(1)} fusion(f32[32,52,128]{2,1,0:T(8,128)S(1)} %slice_bitcast_fusion, f32[32,40,128]{2,1,0:T(8,128)S(1)} %slice.1008, f32[32,40,3]{2,1,0:T(8,128)} %copy.21, f32[32,40,3]{2,1,0:T(8,128)} %copy.19, f32[5,32,52,128]{3,2,1,0:T(8,128)} %copy-done, f32[32,46,128]{2,1,0:T(8,128)S(1)} %fusion.21, ...), kind=kLoop, calls=%fused_computation.299 | loop fusion | flops 69632000 | bytes 8017920 | tf_op jit(solution)/shard_map/add | solution.py:186
  111.7 10.8 %collective-permute-start.10 = (f32[4,40,128]{2,1,0:T(8,128)S(1)}, f32[4,40,128]{2,1,0:T(8,128)S(1)}, u32[]{:S(2)}, u32[]{:S(2)}) collective-permute-start(f32[4,40,128]{2,1,0:T(8,128)S(1)} %get-tuple-element.48), channel_id=1, source_target_pairs={{0,16},{16,32},{32,48},{48,64},{64,80},{80,96},{96,112},{112,128},... | collective-permute-start | bytes 245768 | tf_op jit(solution)/shard_map/ppermute | solution.py:152
  122.5 1.9 %collective-permute-start.11 = (f32[4,40,128]{2,1,0:T(8,128)S(1)}, f32[4,40,128]{2,1,0:T(8,128)S(1)}, u32[]{:S(2)}, u32[]{:S(2)}) collective-permute-start(f32[4,40,128]{2,1,0:T(8,128)S(1)} %get-tuple-element.49), channel_id=1, source_target_pairs={{16,0},{32,16},{48,32},{64,48},{80,64},{96,80},{112,96},{128,112},... | collective-permute-start | bytes 245768 | tf_op jit(solution)/shard_map/ppermute | solution.py:153
  124.5 10.0 %collective-permute-done.11 = f32[4,40,128]{2,1,0:T(8,128)S(1)} collective-permute-done((f32[4,40,128]{2,1,0:T(8,128)S(1)}, f32[4,40,128]{2,1,0:T(8,128)S(1)}, u32[]{:S(2)}, u32[]{:S(2)}) %collective-permute-start.11) | collective-permute-done | bytes 81952 | tf_op jit(solution)/shard_map/ppermute | solution.py:153
  134.5 1.1 fusion.456
  135.6 1.5 copy.22
  137.1 1.9 %collective-permute-start.12 = (f32[34,34,3]{1,0,2:T(8,128)S(1)}, f32[34,34,3]{1,0,2:T(8,128)S(1)}, u32[]{:S(2)}, u32[]{:S(2)}) collective-permute-start(f32[34,34,3]{1,0,2:T(8,128)S(1)} %copy.22), channel_id=1, source_target_pairs={{0,1},{1,2},{2,3},{3,0},{4,5},{5,6},{6,7},{7,4},{8,9},{9,10},{10,1... | collective-permute-start | bytes 41624 | tf_op jit(solution)/shard_map/ppermute | solution.py:61
  139.0 1.0 copy.24
  140.0 5.8 %collective-permute-start.13 = (f32[34,34,3]{1,0,2:T(8,128)}, f32[34,34,3]{1,0,2:T(8,128)S(1)}, u32[]{:S(2)}, u32[]{:S(2)}) collective-permute-start(f32[34,34,3]{1,0,2:T(8,128)} %copy.24), channel_id=1, source_target_pairs={{1,0},{2,1},{3,2},{0,3},{5,4},{6,5},{7,6},{4,7},{9,8},{10,9},{11,1... | collective-permute-start | bytes 41624 | tf_op jit(solution)/shard_map/ppermute | solution.py:62
  147.7 0.9 slice.1059
  149.3 1.5 add_select_fusion
  151.2 13.2 %fusion.181 = f32[32,34,128]{2,1,0:T(8,128)S(1)} fusion(f32[34,34,3]{2,1,0:T(8,128)S(1)} %copy.25, f32[34,34,128]{2,1,0:T(8,128)S(1)} %copy-done.1, f32[34,34,3]{2,1,0:T(8,128)S(1)} %copy.23, f32[5,32,52,128]{3,2,1,0:T(8,128)} %copy-done, f32[32,40,128]{2,1,0:T(8,128)S(1)} %fusion.174, f32[4,40,128]{2,1,0:T(8,128)S(1)} %collective-permute-done.11, ...), kind=kLoop, calls=%fused_computation.308 | loop fusion | flops 59465728 | bytes 10936320 | tf_op jit(solution)/shard_map/jit(_where)/select_n | solution.py:199
  165.2 1.0 multiply_reduce_fusion.7
  166.3 1.0 multiply_reduce_fusion.5
  167.3 1.0 multiply_reduce_fusion.3
  168.4 1.0 multiply_reduce_fusion.1
  169.6 1.3 copy.26
  170.8 1.2 slice_bitcast_fusion.4
  172.0 1.3 copy.27
  173.3 1.3 copy.28
  175.8 3.3 %all-to-all-start = ((f32[4,1,4096]{2,1,0:T(1,128)}), f32[4,1,4096]{2,1,0:T(1,128)S(1)}, u32[]{:S(2)}, u32[]{:S(2)}) async-start(f32[4,1,4096]{2,1,0:T(1,128)} %reshape.128), calls=%async_computation | async-start | bytes 131072 | tf_op jit(solution)/shard_map/all_to_all | solution.py:232
  179.1 0.9 slice.1073
  180.0 3.7 %all-to-all-done = f32[4,1,4096]{2,1,0:T(1,128)S(1)} async-done(((f32[4,1,4096]{2,1,0:T(1,128)}), f32[4,1,4096]{2,1,0:T(1,128)S(1)}, u32[]{:S(2)}, u32[]{:S(2)}) %all-to-all-start) | async-done | bytes 65568 | tf_op jit(solution)/shard_map/all_to_all | solution.py:232
  184.2 0.8 reduce
  (76 shorter events, 12.9 us)
Async XLA Ops:
  0.6 2.8 %copy-start.4 = (bf16[3,32,32,128]{3,2,1,0:T(8,128)(2,1)S(1)}, bf16[3,32,32,128]{3,2,1,0:T(8,128)(2,1)}, u32[]{:S(2)}) copy-start(bf16[3,32,32,128]{3,2,1,0:T(8,128)(2,1)} %param.5) | copy-start | bytes 2359300
  4.1 21.0 %collective-permute-start = (f32[5,32,10,128]{3,1,2,0:T(8,128)S(1)}, f32[5,32,10,128]{3,1,2,0:T(8,128)S(1)}, u32[]{:S(2)}, u32[]{:S(2)}) collective-permute-start(f32[5,32,10,128]{3,1,2,0:T(8,128)S(1)} %copy.10), channel_id=1, source_target_pairs={{0,4},{4,8},{8,12},{12,0},{1,5},{5,9},{9,13},{13,1},{2,6},{6,10},{... | collective-permute-start | bytes 2457608 | tf_op jit(solution)/shard_map/ppermute | solution.py:21
  7.6 20.7 %collective-permute-start.1 = (f32[5,32,10,128]{3,1,2,0:T(8,128)S(1)}, f32[5,32,10,128]{3,1,2,0:T(8,128)S(1)}, u32[]{:S(2)}, u32[]{:S(2)}) collective-permute-start(f32[5,32,10,128]{3,1,2,0:T(8,128)S(1)} %copy.11), channel_id=1, source_target_pairs={{4,0},{8,4},{12,8},{0,12},{5,1},{9,5},{13,9},{1,13},{6,2},{10,6},{... | collective-permute-start | bytes 2457608 | tf_op jit(solution)/shard_map/ppermute | solution.py:22
  29.4 2.1 %copy-start = (f32[5,32,52,128]{3,2,1,0:T(8,128)}, f32[5,32,52,128]{3,2,1,0:T(8,128)S(1)}, u32[]{:S(2)}) copy-start(f32[5,32,52,128]{3,2,1,0:T(8,128)S(1)} %pad_maximum_fusion) | copy-start | bytes 12779524
  33.4 23.0 %collective-permute-start.2 = (f32[7,46,128]{2,1,0:T(8,128)}, f32[7,46,128]{2,1,0:T(8,128)S(1)}, u32[]{:S(2)}, u32[]{:S(2)}) collective-permute-start(f32[7,46,128]{2,1,0:T(8,128)} %get-tuple-element.19), channel_id=1, source_target_pairs={{0,16},{16,32},{32,48},{48,64},{64,80},{80,96},{96,112},{112,128},... | collective-permute-start | bytes 494600 | tf_op jit(solution)/shard_map/ppermute | solution.py:181
  43.8 15.7 %collective-permute-start.3 = (f32[7,46,128]{2,1,0:T(8,128)}, f32[7,46,128]{2,1,0:T(8,128)}, u32[]{:S(2)}, u32[]{:S(2)}) collective-permute-start(f32[7,46,128]{2,1,0:T(8,128)} %get-tuple-element.18), channel_id=1, source_target_pairs={{16,0},{32,16},{48,32},{64,48},{80,64},{96,80},{112,96},{128,112},... | collective-permute-start | bytes 494600 | tf_op jit(solution)/shard_map/ppermute | solution.py:182
  46.4 7.5 %collective-permute-start.4 = (f32[32,46,3]{1,0,2:T(8,128)S(1)}, f32[32,46,3]{1,0,2:T(8,128)S(1)}, u32[]{:S(2)}, u32[]{:S(2)}) collective-permute-start(f32[32,46,3]{1,0,2:T(8,128)S(1)} %copy.14), channel_id=1, source_target_pairs={{0,1},{1,2},{2,3},{3,0},{4,5},{5,6},{6,7},{7,4},{8,9},{9,10},{10,1... | collective-permute-start | bytes 53000 | tf_op jit(solution)/shard_map/ppermute | solution.py:61
  49.4 5.8 %collective-permute-start.5 = (f32[32,46,3]{1,0,2:T(8,128)S(1)}, f32[32,46,3]{1,0,2:T(8,128)S(1)}, u32[]{:S(2)}, u32[]{:S(2)}) collective-permute-start(f32[32,46,3]{1,0,2:T(8,128)S(1)} %copy.16), channel_id=1, source_target_pairs={{1,0},{2,1},{3,2},{0,3},{5,4},{6,5},{7,6},{4,7},{9,8},{10,9},{11,1... | collective-permute-start | bytes 53000 | tf_op jit(solution)/shard_map/ppermute | solution.py:62
  75.4 23.2 %collective-permute-start.6 = (f32[3,40,128]{2,1,0:T(8,128)S(1)}, f32[3,40,128]{2,1,0:T(8,128)S(1)}, u32[]{:S(2)}, u32[]{:S(2)}) collective-permute-start(f32[3,40,128]{2,1,0:T(8,128)S(1)} %get-tuple-element.39), channel_id=1, source_target_pairs={{0,16},{16,32},{32,48},{48,64},{64,80},{80,96},{96,112},{112,128},... | collective-permute-start | bytes 184328 | tf_op jit(solution)/shard_map/ppermute | solution.py:152
  85.5 13.1 %collective-permute-start.7 = (f32[3,40,128]{2,1,0:T(8,128)S(1)}, f32[3,40,128]{2,1,0:T(8,128)S(1)}, u32[]{:S(2)}, u32[]{:S(2)}) collective-permute-start(f32[3,40,128]{2,1,0:T(8,128)S(1)} %get-tuple-element.38), channel_id=1, source_target_pairs={{16,0},{32,16},{48,32},{64,48},{80,64},{96,80},{112,96},{128,112},... | collective-permute-start | bytes 184328 | tf_op jit(solution)/shard_map/ppermute | solution.py:153
  88.0 8.1 %collective-permute-start.8 = (f32[32,40,3]{1,0,2:T(8,128)S(1)}, f32[32,40,3]{1,0,2:T(8,128)S(1)}, u32[]{:S(2)}, u32[]{:S(2)}) collective-permute-start(f32[32,40,3]{1,0,2:T(8,128)S(1)} %copy.18), channel_id=1, source_target_pairs={{0,1},{1,2},{2,3},{3,0},{4,5},{5,6},{6,7},{7,4},{8,9},{9,10},{10,1... | collective-permute-start | bytes 46088 | tf_op jit(solution)/shard_map/ppermute | solution.py:61
  90.8 6.6 %collective-permute-start.9 = (f32[32,40,3]{1,0,2:T(8,128)}, f32[32,40,3]{1,0,2:T(8,128)S(1)}, u32[]{:S(2)}, u32[]{:S(2)}) collective-permute-start(f32[32,40,3]{1,0,2:T(8,128)} %copy.20), channel_id=1, source_target_pairs={{1,0},{2,1},{3,2},{0,3},{5,4},{6,5},{7,6},{4,7},{9,8},{10,9},{11,1... | collective-permute-start | bytes 46088 | tf_op jit(solution)/shard_map/ppermute | solution.py:62
  111.7 12.8 %collective-permute-start.10 = (f32[4,40,128]{2,1,0:T(8,128)S(1)}, f32[4,40,128]{2,1,0:T(8,128)S(1)}, u32[]{:S(2)}, u32[]{:S(2)}) collective-permute-start(f32[4,40,128]{2,1,0:T(8,128)S(1)} %get-tuple-element.48), channel_id=1, source_target_pairs={{0,16},{16,32},{32,48},{48,64},{64,80},{80,96},{96,112},{112,128},... | collective-permute-start | bytes 245768 | tf_op jit(solution)/shard_map/ppermute | solution.py:152
  122.5 12.0 %collective-permute-start.11 = (f32[4,40,128]{2,1,0:T(8,128)S(1)}, f32[4,40,128]{2,1,0:T(8,128)S(1)}, u32[]{:S(2)}, u32[]{:S(2)}) collective-permute-start(f32[4,40,128]{2,1,0:T(8,128)S(1)} %get-tuple-element.49), channel_id=1, source_target_pairs={{16,0},{32,16},{48,32},{64,48},{80,64},{96,80},{112,96},{128,112},... | collective-permute-start | bytes 245768 | tf_op jit(solution)/shard_map/ppermute | solution.py:153
  134.5 11.3 %copy-start.5 = (s32[4]{0:T(128)S(1)}, s32[4]{0:T(128)}, u32[]{:S(2)}) copy-start(s32[4]{0:T(128)} %param.7) | copy-start | bytes 52
  137.1 11.5 %collective-permute-start.12 = (f32[34,34,3]{1,0,2:T(8,128)S(1)}, f32[34,34,3]{1,0,2:T(8,128)S(1)}, u32[]{:S(2)}, u32[]{:S(2)}) collective-permute-start(f32[34,34,3]{1,0,2:T(8,128)S(1)} %copy.22), channel_id=1, source_target_pairs={{0,1},{1,2},{2,3},{3,0},{4,5},{5,6},{6,7},{7,4},{8,9},{9,10},{10,1... | collective-permute-start | bytes 41624 | tf_op jit(solution)/shard_map/ppermute | solution.py:61
  140.0 8.9 %collective-permute-start.13 = (f32[34,34,3]{1,0,2:T(8,128)}, f32[34,34,3]{1,0,2:T(8,128)S(1)}, u32[]{:S(2)}, u32[]{:S(2)}) collective-permute-start(f32[34,34,3]{1,0,2:T(8,128)} %copy.24), channel_id=1, source_target_pairs={{1,0},{2,1},{3,2},{0,3},{5,4},{6,5},{7,6},{4,7},{9,8},{10,9},{11,1... | collective-permute-start | bytes 41624 | tf_op jit(solution)/shard_map/ppermute | solution.py:62
  149.3 1.5 copy-start.1
  164.4 0.8 copy-start.2
  172.0 7.1 %copy-start.3 = (f32[32,34,128]{2,1,0:T(8,128)S(1)}, f32[32,34,128]{2,1,0:T(8,128)}, u32[]{:S(2)}) copy-start(f32[32,34,128]{2,1,0:T(8,128)} %copy-done.2) | copy-start | bytes 1671172
  175.8 7.9 %all-to-all-start = ((f32[4,1,4096]{2,1,0:T(1,128)}), f32[4,1,4096]{2,1,0:T(1,128)S(1)}, u32[]{:S(2)}, u32[]{:S(2)}) async-start(f32[4,1,4096]{2,1,0:T(1,128)} %reshape.128), calls=%async_computation | async-start | bytes 131072 | tf_op jit(solution)/shard_map/all_to_all | solution.py:232
